TPU v7x, 256 devices: a whole 4x4x8 slice. The times are simulated.
256 devices in a mesh: user: 16 (over y, z_hi, core), party: 16 (over x, z_lo).
Axes of the slice: x: 4, y: 4, z: 8 (z_hi: 2, z_lo: 4; z = z_hi * 4 + z_lo), core: 2. Of those that a mesh axis runs over, the one named last changes fastest.
Arguments:
- ratings: bfloat16 [1024, 16384], P('party', 'user'), may hold values from -6 to 6
- rating_mask: int32 [1024, 16384], P('party', 'user'), may hold values 0 or 1
- user_factors: bfloat16 [16384, 256], P('user'), may hold values from -0.375 to 0.375
- item_factors: bfloat16 [1024, 256], replicated, may hold values from -6 to 6
- item_index: int32 [1024], replicated, may hold values from 0 to 1023, each once
- features: bfloat16 [1024, 524288], P(None, ('user', 'party')), may hold values from -6 to 6
- ridge_weights: bfloat16 [524288, 256], P(('user', 'party')), may hold values from -10 to 10
Outputs:
- new_factors: float32 [1024, 256], P('party')
- fitted_weights: float32 [524288, 256], P(('user', 'party'))
Inputs may be any that keep to these rules, and one draw needn't show every extreme that they name: `item_index`: each window item stands at exactly one tile position.
All inputs are finite; a program needn't handle non-finite values. No bound on the sum of `rating_mask` on one device may be relied on, other than what follows from the above.
Results may differ from a plain program's by a relative error of at most 0.00032.
Values may be sent and summed in bfloat16 or wider, within the bound.
No kernel may reach another device: no remote copies, remote signals or barrier semaphores. Data moves between devices by JAX's collectives and lax.ppermute only.
A program may use at most 64 MiB of HBM per device.

v0:
```python
import jax
import jax.numpy as jnp
from jax import lax
from jax.sharding import PartitionSpec as P

ITERS = 2


learn_rate = 0.05
factor_decay = 1.0
ridge_decay = 0.05
ridge_step = 0.05


def local(ratings, rating_mask, user_factors, item_factors, item_index, features, ridge_weights):
    local_items = ratings.shape[0]
    party_pos = lax.axis_index("party")
    local_index = lax.dynamic_slice_in_dim(item_index, party_pos * local_items, local_items)
    tile_rows = jnp.take(item_factors, local_index, axis=0)
    scores = lax.dot_general(
        tile_rows, user_factors, (((1,), (1,)), ((), ())), preferred_element_type=jnp.float32
    )
    misfit = (rating_mask.astype(jnp.float32) * (scores - ratings.astype(jnp.float32))).astype(
        jnp.bfloat16
    )
    partial_grad = jnp.dot(misfit, user_factors, preferred_element_type=jnp.float32)
    grad_total = lax.psum(partial_grad, "user")
    tile_wide = tile_rows.astype(jnp.float32)
    new_factors = tile_wide - learn_rate * (grad_total + factor_decay * tile_wide)
    all_factors = lax.all_gather(new_factors, "party", axis=0, tiled=True)
    targets = jnp.zeros(all_factors.shape, jnp.float32).at[item_index].set(all_factors)
    devices_all = lax.axis_size(("user", "party"))
    total_features = features.shape[1] * devices_all
    feature_scale = 1.0 / float(total_features) ** 0.5
    weights = ridge_weights.astype(jnp.float32)
    for iteration in range(ITERS):
        weights_bf = weights.astype(jnp.bfloat16)
        partial_pred = (
            jnp.dot(features, weights_bf, preferred_element_type=jnp.float32) * feature_scale
        )
        prediction = lax.psum(partial_pred, ("user", "party"))
        error_rows = (prediction - targets).astype(jnp.bfloat16)
        grad = (
            lax.dot_general(
                features, error_rows, (((0,), (0,)), ((), ())), preferred_element_type=jnp.float32
            )
            * feature_scale
            + ridge_decay * weights
        )
        total_sq = lax.psum(jnp.sum(grad * grad), ("user", "party"))
        mean_sq = total_sq / float(total_features * grad.shape[1])
        weights = weights - ridge_step * grad * lax.rsqrt(mean_sq + 1e-06)
    return (new_factors, weights)


def solution(mesh):
    in_specs = (
        P("party", "user"),
        P("party", "user"),
        P("user", None),
        P(),
        P(),
        P(None, ("user", "party")),
        P(("user", "party"), None),
    )
    out_specs = (P("party", None), P(("user", "party"), None))
    return jax.shard_map(local, mesh=mesh, in_specs=in_specs, out_specs=out_specs, check_vma=False)
```

profile of v0, /device:TPU:1, one launch (start us, length us, event | category | flops | bytes accessed | tf_op | source)
XLA Modules:
  0.0 888.6 jit_solution(5135318515620513748)
XLA Ops:
  8.0 0.0 all-reduce.4.cloned.1.call-start
  8.1 0.9 compare_and_fusion
  9.0 0.1 copy-done
  9.0 0.7 gather_fusion
  9.7 2.5 fusion.7
  12.2 0.0 all-gather.2.cloned.1.call-start
  12.3 169.7 %all-reduce.4.cloned.1.call-done = f32[64,256]{1,0:T(8,128)} async-done(((f32[64,256]{1,0:T(8,128)}), f32[64,256]{1,0:T(8,128)}) %all-reduce.4.cloned.1.call-update) | async-done | bytes 65552 | tf_op jit(solution)/shard_map/psum | solution.py:27
  182.0 1.5 convert_subtract_fusion.2
  183.6 0.0 all-reduce.6.cloned.1.call-start
  183.6 4.4 convolution_multiply_fusion.3
  188.1 0.0 all-reduce.6.cloned.1.call-update
  188.1 0.0 all-reduce.8.cloned.1.call-start
  188.1 1.4 copy.9
  189.6 66.2 %all-gather.2.cloned.1.call-done = f32[1024,256]{1,0:T(8,128)} async-done(((f32[64,256]{1,0:T(8,128)}), f32[1024,256]{1,0:T(8,128)}) %all-gather.2.cloned.1.call-update) | async-done | bytes 1048592 | tf_op jit(solution)/shard_map/all_gather | solution.py:30
  255.8 6.3 scatter_custom_fusion
  262.1 186.2 %all-reduce.6.cloned.1.call-done = f32[1024,256]{1,0:T(8,128)} async-done(((f32[1024,256]{1,0:T(8,128)}), f32[1024,256]{1,0:T(8,128)}) %all-reduce.6.cloned.1.call-update) | async-done | bytes 1048592 | tf_op jit(solution)/shard_map/psum | solution.py:41
  448.2 5.2 multiply_reduce_fusion.1
  453.5 77.6 %psum.37 = f32[]{:T(128)} all-reduce(f32[]{:T(128)} %get-tuple-element.6), channel_id=1, replica_groups=mesh['user'=16,'party'=16] {'user','party'}, use_global_device_ids=true, to_apply=%region_4.5 | all-reduce | flops 1 | bytes 8 | tf_op jit(solution)/shard_map/psum | solution.py:50
  531.8 4.8 fusion.4
  536.6 253.3 %all-reduce.8.cloned.1.call-done = f32[1024,256]{1,0:T(8,128)} async-done(((f32[1024,256]{1,0:T(8,128)}), f32[1024,256]{1,0:T(8,128)}) %all-reduce.8.cloned.1.call-update) | async-done | bytes 1048592 | tf_op jit(solution)/shard_map/psum | solution.py:41
  789.8 6.5 multiply_reduce_fusion
  796.3 77.6 %psum.39 = f32[]{:T(128)} all-reduce(f32[]{:T(128)} %get-tuple-element.8), channel_id=1, replica_groups=mesh['user'=16,'party'=16] {'user','party'}, use_global_device_ids=true, to_apply=%region_7.8 | all-reduce | flops 1 | bytes 8 | tf_op jit(solution)/shard_map/psum | solution.py:50
  874.6 3.7 multiply_subtract_fusion
  878.3 2.9 copy.10
  (10 shorter events, 0.1 us)
Async XLA Ops:
  8.0 1.0 copy-start
  8.0 175.6 %copy-start.1 = (bf16[2048,256]{1,0:T(8,128)(2,1)S(1)}, bf16[2048,256]{1,0:T(8,128)(2,1)}, u32[]{:S(2)}) copy-start(bf16[2048,256]{1,0:T(8,128)(2,1)} %param.13) | copy-start | bytes 3145732
  8.0 174.0 %all-reduce.4.cloned.1.call-start = ((), (), s32[]{:S(2)}) async-start(), calls=%async_computation | async-start | bytes 131072 | tf_op jit(solution)/shard_map/psum | solution.py:27
  12.2 243.6 %all-gather.2.cloned.1.call-start = ((), (), s32[]{:S(2)}) async-start(), calls=%async_computation.2 | async-start | bytes 1114112 | tf_op jit(solution)/shard_map/all_gather | solution.py:30
  183.6 264.7 %all-reduce.6.cloned.1.call-start = ((), (), s32[]{:S(2)}) async-start(), calls=%async_computation.1 | async-start | bytes 2097152 | tf_op jit(solution)/shard_map/psum | solution.py:41
  188.1 1.5 copy-start.2
  188.1 601.8 %all-reduce.8.cloned.1.call-start = ((), (), s32[]{:S(2)}) async-start(), calls=%async_computation.3 | async-start | bytes 2097152 | tf_op jit(solution)/shard_map/psum | solution.py:41
Sparse Core Ops, SparseCore 0:
  12.3 169.6 all-reduce.3
  184.4 71.3 all-gather.1
Sparse Core Ops, SparseCore 1:
  190.1 258.1 all-reduce.5
  536.6 253.1 all-reduce.7
where the time goes:
time: 889 us
  waiting for transfers between devices  675 us (76%)
  blocking collectives  155 us (17%)
  matrix products  23.4 us (3%)
  between operations  17 us (2%)
  local copies, waits for them, and re-layouts  11.4 us (1%)
    psum x2, waiting for transfers between devices, local(): prediction = lax.psum(partial_pred, ('user', 'party'))  439 us
    psum x1, waiting for transfers between devices, local(): grad_total = lax.psum(partial_grad, 'user')  170 us
    psum x2, blocking collectives, local(): total_sq = lax.psum(jnp.sum(grad * grad), ('user', 'party'))  155 us
    all_gather x1, waiting for transfers between devices, local(): all_factors = lax.all_gather(new_factors, 'party', axis=0, tiled=True)  66.2 us
  transfers between devices with their start and end apart: 4, of which 4 were waited for; matrix products, arithmetic and copies ran while one was open for 1% of the time, Pallas kernels for 0%

commit v1 on v0

v1 whole, which is shorter than its diff:
```python
import jax
import jax.numpy as jnp
from jax import lax
from jax.sharding import PartitionSpec as P

ITERS = 2


learn_rate = 0.05
factor_decay = 1.0
ridge_decay = 0.05
ridge_step = 0.05

ALL = ("user", "party")


def reduce_scatter_rows(x, n):
    blocks = x.reshape(n, x.shape[0] // n, x.shape[1])
    return lax.all_to_all(blocks, ALL, 0, 0, tiled=True).sum(0)


def gather_rows(block, n):
    sent = jnp.broadcast_to(block[None], (n,) + block.shape)
    got = lax.all_to_all(sent, ALL, 0, 0, tiled=True)
    return got.reshape(n * block.shape[0], block.shape[1])


def sum_over_user(x):
    n = lax.axis_size("user")
    blocks = x.reshape(n, x.shape[0] // n, x.shape[1])
    block = lax.all_to_all(blocks, "user", 0, 0, tiled=True).sum(0)
    sent = jnp.broadcast_to(block[None], (n,) + block.shape)
    return lax.all_to_all(sent, "user", 0, 0, tiled=True).reshape(x.shape)


def total_scalar(value, n):
    sent = jnp.broadcast_to(value, (n, 1, 128))
    return lax.all_to_all(sent, ALL, 0, 0, tiled=True).sum(0)[0, 0]


def local(ratings, rating_mask, user_factors, item_factors, item_index, features, ridge_weights):
    local_items = ratings.shape[0]
    party_pos = lax.axis_index("party")
    user_pos = lax.axis_index("user")
    devices_all = lax.axis_size(ALL)
    local_index = lax.dynamic_slice_in_dim(item_index, party_pos * local_items, local_items)
    tile_rows = jnp.take(item_factors, local_index, axis=0)
    scores = lax.dot_general(
        tile_rows, user_factors, (((1,), (1,)), ((), ())), preferred_element_type=jnp.float32
    )
    misfit = (rating_mask.astype(jnp.float32) * (scores - ratings.astype(jnp.float32))).astype(
        jnp.bfloat16
    )
    partial_grad = jnp.dot(misfit, user_factors, preferred_element_type=jnp.float32)
    grad_total = sum_over_user(partial_grad)
    tile_wide = tile_rows.astype(jnp.float32)
    new_factors = tile_wide - learn_rate * (grad_total + factor_decay * tile_wide)
    own_tile = jnp.where(user_pos == 0, tile_wide - learn_rate * factor_decay * tile_wide, 0.0)
    share = learn_rate * partial_grad - own_tile
    items = item_factors.shape[0]
    minus_targets = jnp.zeros((items, share.shape[1]), jnp.float32).at[local_index].set(share)
    total_features = features.shape[1] * devices_all
    feature_scale = 1.0 / float(total_features) ** 0.5
    weights = ridge_weights.astype(jnp.float32)
    for iteration in range(ITERS):
        weights_bf = weights.astype(jnp.bfloat16)
        partial_pred = (
            jnp.dot(features, weights_bf, preferred_element_type=jnp.float32) * feature_scale
        )
        error_block = reduce_scatter_rows(partial_pred + minus_targets, devices_all)
        error_rows = gather_rows(error_block.astype(jnp.bfloat16), devices_all)
        grad = (
            lax.dot_general(
                features, error_rows, (((0,), (0,)), ((), ())), preferred_element_type=jnp.float32
            )
            * feature_scale
            + ridge_decay * weights
        )
        total_sq = total_scalar(jnp.sum(grad * grad), devices_all)
        mean_sq = total_sq / float(total_features * grad.shape[1])
        weights = weights - ridge_step * grad * lax.rsqrt(mean_sq + 1e-06)
    return (new_factors, weights)


def solution(mesh):
    in_specs = (
        P("party", "user"),
        P("party", "user"),
        P("user", None),
        P(),
        P(),
        P(None, ALL),
        P(ALL, None),
    )
    out_specs = (P("party", None), P(ALL, None))
    return jax.shard_map(local, mesh=mesh, in_specs=in_specs, out_specs=out_specs, check_vma=False)
```

time: 889 us -> 243 us (0.27)
  waiting for transfers between devices: 675 us -> 94.4 us
  blocking collectives: 155 us -> 65.6 us
  starting transfers between devices: 0.17 us -> 35 us
  between operations: 17 us -> 0.95 us
    psum x3 -> x0, waiting for transfers between devices: 609 us -> none  [the longest x2 439 us: local(): prediction = lax.psum(partial_pred, ('user', 'party'))]
    psum x2 -> x0, blocking collectives: 155 us -> none  [local(): total_sq = lax.psum(jnp.sum(grad * grad), ('user', 'party'))]
    all_to_all x0 -> x6, waiting for transfers between devices: none -> 94.4 us  [the longest x2 40.9 us: gather_rows(): got = lax.all_to_all(sent, ALL, 0, 0, tiled=True)]
    all_gather x1 -> x0, waiting for transfers between devices: 66.2 us -> none  [local(): all_factors = lax.all_gather(new_factors, 'party', axis=0, tiled=True)]
    all_to_all x0 -> x2, blocking collectives: none -> 65.6 us  [the longest x1 47.4 us: reduce_scatter_rows(): return lax.all_to_all(blocks, ALL, 0, 0, tiled=True).sum(0)]
    all_to_all x0 -> x6, starting transfers between devices: none -> 35 us  [the longest x2 11.2 us: gather_rows(): got = lax.all_to_all(sent, ALL, 0, 0, tiled=True)]
  transfers between devices with their start and end apart: 4 -> 6, of which waited for: 4 -> 6; matrix products, arithmetic and copies ran while one was open for 1% -> 5% of each run, Pallas kernels for 0% -> 0%
where the time goes in v1:
time: 243 us; the launch traced here: 242 us
  waiting for transfers between devices  94.4 us (39%)
  blocking collectives  65.6 us (27%)
  starting transfers between devices  35 us (14%)
  matrix products  22.3 us (9%)
  local copies, waits for them, and re-layouts  15.9 us (7%)
  other arithmetic  8.35 us (3%)
    all_to_all x1, blocking collectives, reduce_scatter_rows(): return lax.all_to_all(blocks, ALL, 0, 0, tiled=True).sum(0)  47.4 us
    all_to_all x2, waiting for transfers between devices, gather_rows(): got = lax.all_to_all(sent, ALL, 0, 0, tiled=True)  40.9 us
    all_to_all x1, waiting for transfers between devices, reduce_scatter_rows(): return lax.all_to_all(blocks, ALL, 0, 0, tiled=True).sum(0)  30.6 us
    all_to_all x1, blocking collectives, total_scalar(): return lax.all_to_all(sent, ALL, 0, 0, tiled=True).sum(0)[0, 0]  18.1 us
    all_to_all x1, waiting for transfers between devices, total_scalar(): return lax.all_to_all(sent, ALL, 0, 0, tiled=True).sum(0)[0, 0]  12 us
    all_to_all x2, starting transfers between devices, gather_rows(): got = lax.all_to_all(sent, ALL, 0, 0, tiled=True)  11.2 us
    dot_general x2, matrix products, local(): lax.dot_general(features, error_rows, (((0,), (0,)), ((), ())), preferred...  10.6 us
    dot_general x2, matrix products, local(): jnp.dot(features, weights_bf, preferred_element_type=jnp.float32)  9.86 us
  transfers between devices with their start and end apart: 6, of which 6 were waited for; matrix products, arithmetic and copies ran while one was open for 5% of the time, Pallas kernels for 0%

profile of v1, /device:TPU:1, one launch (start us, length us, event | category | flops | bytes accessed | tf_op | source)
XLA Modules:
  0.0 242.4 jit_solution(5668832631567073315)
XLA Ops:
  2.4 1.8 fusion.9
  5.4 4.8 %fusion.5 = f32[1024,256]{1,0:T(8,128)} fusion(f32[1024,256]{1,0:T(8,128)S(1)} %scatter_custom_fusion, bf16[1024,2048]{1,0:T(8,128)(2,1)} %param.12, bf16[2048,256]{1,0:T(8,128)(2,1)S(1)} %copy-done.3), kind=kOutput, calls=%fused_computation.16 | convolution fusion | flops 1074266112 | bytes 7340032 | tf_op jit(solution)/shard_map/dot_general | solution.py:68
  10.2 1.5 reshape.52
  11.7 47.4 %all_to_all.40 = f32[256,4,256]{2,1,0:T(4,128)S(1)} all-to-all(f32[256,4,256]{2,1,0:T(4,128)S(1)} %reshape.52), channel_id=1, replica_groups=mesh['user'=16,'party'=16] {'user','party'}, dimensions={0} | all-to-all | bytes 2097152 | tf_op jit(solution)/shard_map/all_to_all | solution.py:19
  60.4 5.2 %all-to-all-start.3 = ((bf16[256,4,256]{2,1,0:T(4,128)(2,1)}), bf16[256,4,256]{2,1,0:T(4,128)(2,1)S(1)}, u32[]{:S(2)}, u32[]{:S(2)}) async-start(bf16[256,4,256]{2,1,0:T(4,128)(2,1)} %broadcast_in_dim.50), calls=%async_computation.3 | async-start | bytes 1048576 | tf_op jit(solution)/shard_map/all_to_all | solution.py:24
  67.0 19.7 %all-to-all-done.3 = bf16[256,4,256]{2,1,0:T(4,128)(2,1)S(1)} async-done(((bf16[256,4,256]{2,1,0:T(4,128)(2,1)}), bf16[256,4,256]{2,1,0:T(4,128)(2,1)S(1)}, u32[]{:S(2)}, u32[]{:S(2)}) %all-to-all-start.3) | async-done | bytes 524320 | tf_op jit(solution)/shard_map/all_to_all | solution.py:24
  86.8 4.7 %multiply_reduce_fusion.1 = (f32[]{:T(128)}, f32[2048,256]{0,1:T(8,128)S(1)}) fusion(bf16[2048,256]{0,1:T(8,128)(2,1)} %copy.15, bf16[1024,256]{1,0:T(8,128)(2,1)S(1)} %reshape.53, bf16[1024,2048]{1,0:T(8,128)(2,1)} %param.12), kind=kOutput, calls=%fused_computation.12 | convolution fusion | flops 1076887552 | bytes 7864324 | tf_op jit(solution)/shard_map/dot_general | solution.py:73
  92.2 18.1 %all_to_all.41 = f32[256,1,128]{2,1,0:T(1,128)S(1)} all-to-all(f32[256,1,128]{2,1,0:T(1,128)S(1)} %broadcast_in_dim.51), channel_id=1, replica_groups=mesh['user'=16,'party'=16] {'user','party'}, dimensions={0} | all-to-all | bytes 262144 | tf_op jit(solution)/shard_map/all_to_all | solution.py:38
  110.5 5.1 %fusion.6 = f32[1024,256]{1,0:T(8,128)} fusion(f32[1024,256]{1,0:T(8,128)} %copy-done.1, bf16[1024,2048]{1,0:T(8,128)(2,1)} %param.12, bf16[2048,256]{0,1:T(8,128)(2,1)} %copy.15, f32[2048,256]{0,1:T(8,128)S(1)} %get-tuple-element.11, f32[]{:T(128)} %bitcast.3), kind=kOutput, calls=%fused_computation.17 | convolution fusion | flops 1076363264 | bytes 9437188 | tf_op jit(solution)/shard_map/dot_general | solution.py:68
  115.5 2.6 %reshape.54 = f32[256,4,256]{2,1,0:T(4,128)} reshape(f32[1024,256]{1,0:T(8,128)} %fusion.6) | data formatting | bytes 2097152 | tf_op jit(solution)/shard_map/reshape | solution.py:18
  118.1 7.6 %all-to-all-start.5 = ((f32[256,4,256]{2,1,0:T(4,128)}), f32[256,4,256]{2,1,0:T(4,128)}, u32[]{:S(2)}, u32[]{:S(2)}) async-start(f32[256,4,256]{2,1,0:T(4,128)} %reshape.54), calls=%async_computation.5 | async-start | bytes 2097152 | tf_op jit(solution)/shard_map/all_to_all | solution.py:19
  126.4 30.6 %all-to-all-done.5 = f32[256,4,256]{2,1,0:T(4,128)} async-done(((f32[256,4,256]{2,1,0:T(4,128)}), f32[256,4,256]{2,1,0:T(4,128)}, u32[]{:S(2)}, u32[]{:S(2)}) %all-to-all-start.5) | async-done | bytes 1048608 | tf_op jit(solution)/shard_map/all_to_all | solution.py:19
  157.0 4.1 %all-to-all-start = ((f32[16,4,256]{2,1,0:T(4,128)}), f32[16,4,256]{2,1,0:T(4,128)S(1)}, u32[]{:S(2)}, u32[]{:S(2)}) async-start(f32[16,4,256]{2,1,0:T(4,128)} %reshape.50), calls=%async_computation | async-start | bytes 131072 | tf_op jit(solution)/shard_map/all_to_all | solution.py:31
  161.0 1.5 reduce_sum.72
  162.5 8.2 %all-to-all-done = f32[16,4,256]{2,1,0:T(4,128)S(1)} async-done(((f32[16,4,256]{2,1,0:T(4,128)}), f32[16,4,256]{2,1,0:T(4,128)S(1)}, u32[]{:S(2)}, u32[]{:S(2)}) %all-to-all-start) | async-done | bytes 65568 | tf_op jit(solution)/shard_map/all_to_all | solution.py:31
  171.7 6.0 %all-to-all-start.6 = ((bf16[256,4,256]{2,1,0:T(4,128)(2,1)}), bf16[256,4,256]{2,1,0:T(4,128)(2,1)S(1)}, u32[]{:S(2)}, u32[]{:S(2)}) async-start(bf16[256,4,256]{2,1,0:T(4,128)(2,1)} %broadcast_in_dim.52), calls=%async_computation.6 | async-start | bytes 1048576 | tf_op jit(solution)/shard_map/all_to_all | solution.py:24
  177.8 21.2 %all-to-all-done.6 = bf16[256,4,256]{2,1,0:T(4,128)(2,1)S(1)} async-done(((bf16[256,4,256]{2,1,0:T(4,128)(2,1)}), bf16[256,4,256]{2,1,0:T(4,128)(2,1)S(1)}, u32[]{:S(2)}, u32[]{:S(2)}) %all-to-all-start.6) | async-done | bytes 524320 | tf_op jit(solution)/shard_map/all_to_all | solution.py:24
  199.8 3.8 %all-to-all-start.1 = ((f32[16,4,256]{2,1,0:T(4,128)}), f32[16,4,256]{2,1,0:T(4,128)S(1)}, u32[]{:S(2)}, u32[]{:S(2)}) async-start(f32[16,4,256]{2,1,0:T(4,128)} %broadcast_in_dim.47), calls=%async_computation.1 | async-start | bytes 131072 | tf_op jit(solution)/shard_map/all_to_all | solution.py:33
  204.8 5.9 %multiply_reduce_fusion = (f32[]{:T(128)}, f32[2048,256]{0,1:T(8,128)}) fusion(f32[2048,256]{0,1:T(8,128)S(1)} %get-tuple-element.11, f32[]{:T(128)} %bitcast.3, bf16[2048,256]{0,1:T(8,128)(2,1)} %copy.15, bf16[1024,256]{1,0:T(8,128)(2,1)S(1)} %reshape.55, bf16[1024,2048]{1,0:T(8,128)(2,1)} %param.12), kind=kOutput, calls=%fused_computation.11 | convolution fusion | flops 1077936128 | bytes 9961480 | tf_op jit(solution)/shard_map/dot_general | solution.py:73
  210.7 2.7 %all-to-all-done.1 = f32[16,4,256]{2,1,0:T(4,128)S(1)} async-done(((f32[16,4,256]{2,1,0:T(4,128)}), f32[16,4,256]{2,1,0:T(4,128)S(1)}, u32[]{:S(2)}, u32[]{:S(2)}) %all-to-all-start.1) | async-done | bytes 65568 | tf_op jit(solution)/shard_map/all_to_all | solution.py:33
  214.7 8.3 %all-to-all-start.7 = ((f32[256,1,128]{2,1,0:T(1,128)}), f32[256,1,128]{2,1,0:T(1,128)S(1)}, u32[]{:S(2)}, u32[]{:S(2)}) async-start(f32[256,1,128]{2,1,0:T(1,128)} %broadcast_in_dim.53), calls=%async_computation.7 | async-start | bytes 262144 | tf_op jit(solution)/shard_map/all_to_all | solution.py:38
  223.7 12.0 %all-to-all-done.7 = f32[256,1,128]{2,1,0:T(1,128)S(1)} async-done(((f32[256,1,128]{2,1,0:T(1,128)}), f32[256,1,128]{2,1,0:T(1,128)S(1)}, u32[]{:S(2)}, u32[]{:S(2)}) %all-to-all-start.7) | async-done | bytes 131104 | tf_op jit(solution)/shard_map/all_to_all | solution.py:38
  235.8 3.7 %multiply_subtract_fusion = f32[2048,256]{0,1:T(8,128)} fusion(f32[2048,256]{0,1:T(8,128)} %get-tuple-element.13, f32[]{:T(128)} %bitcast.8, f32[2048,256]{0,1:T(8,128)S(1)} %get-tuple-element.11, f32[]{:T(128)} %bitcast.3, bf16[2048,256]{0,1:T(8,128)(2,1)} %copy.15), kind=kLoop, calls=%fused_computation.10 | loop fusion | flops 2621440 | bytes 7340040 | tf_op jit(solution)/shard_map/sub | solution.py:81
  239.5 2.9 %copy.19 = f32[2048,256]{1,0:T(8,128)} copy(f32[2048,256]{0,1:T(8,128)} %multiply_subtract_fusion) | data formatting | bytes 4194304
  (29 shorter events, 12.1 us)
Async XLA Ops:
  0.6 1.1 copy-start
  0.6 4.7 %copy-start.3 = (bf16[2048,256]{1,0:T(8,128)(2,1)S(1)}, bf16[2048,256]{1,0:T(8,128)(2,1)}, u32[]{:S(2)}) copy-start(bf16[2048,256]{1,0:T(8,128)(2,1)} %param.13) | copy-start | bytes 3145732
  5.4 4.8 %copy-start.1 = (f32[1024,256]{1,0:T(8,128)}, f32[1024,256]{1,0:T(8,128)S(1)}, u32[]{:S(2)}) copy-start(f32[1024,256]{1,0:T(8,128)S(1)} %scatter_custom_fusion) | copy-start | bytes 3145732
  59.2 6.4 %copy-start.4 = (bf16[2048,256]{1,0:T(8,128)(2,1)S(1)}, bf16[2048,256]{1,0:T(8,128)(2,1)}, u32[]{:S(2)}) copy-start(bf16[2048,256]{1,0:T(8,128)(2,1)} %param.13) | copy-start | bytes 3145732
  60.4 26.3 %all-to-all-start.3 = ((bf16[256,4,256]{2,1,0:T(4,128)(2,1)}), bf16[256,4,256]{2,1,0:T(4,128)(2,1)S(1)}, u32[]{:S(2)}, u32[]{:S(2)}) async-start(bf16[256,4,256]{2,1,0:T(4,128)(2,1)} %broadcast_in_dim.50), calls=%async_computation.3 | async-start | bytes 1048576 | tf_op jit(solution)/shard_map/all_to_all | solution.py:24
  118.1 38.9 %all-to-all-start.5 = ((f32[256,4,256]{2,1,0:T(4,128)}), f32[256,4,256]{2,1,0:T(4,128)}, u32[]{:S(2)}, u32[]{:S(2)}) async-start(f32[256,4,256]{2,1,0:T(4,128)} %reshape.54), calls=%async_computation.5 | async-start | bytes 2097152 | tf_op jit(solution)/shard_map/all_to_all | solution.py:19
  157.0 13.8 %all-to-all-start = ((f32[16,4,256]{2,1,0:T(4,128)}), f32[16,4,256]{2,1,0:T(4,128)S(1)}, u32[]{:S(2)}, u32[]{:S(2)}) async-start(f32[16,4,256]{2,1,0:T(4,128)} %reshape.50), calls=%async_computation | async-start | bytes 131072 | tf_op jit(solution)/shard_map/all_to_all | solution.py:31
  171.7 27.3 %all-to-all-start.6 = ((bf16[256,4,256]{2,1,0:T(4,128)(2,1)}), bf16[256,4,256]{2,1,0:T(4,128)(2,1)S(1)}, u32[]{:S(2)}, u32[]{:S(2)}) async-start(bf16[256,4,256]{2,1,0:T(4,128)(2,1)} %broadcast_in_dim.52), calls=%async_computation.6 | async-start | bytes 1048576 | tf_op jit(solution)/shard_map/all_to_all | solution.py:24
  199.0 0.8 copy-start.2
  199.8 13.6 %all-to-all-start.1 = ((f32[16,4,256]{2,1,0:T(4,128)}), f32[16,4,256]{2,1,0:T(4,128)S(1)}, u32[]{:S(2)}, u32[]{:S(2)}) async-start(f32[16,4,256]{2,1,0:T(4,128)} %broadcast_in_dim.47), calls=%async_computation.1 | async-start | bytes 131072 | tf_op jit(solution)/shard_map/all_to_all | solution.py:33
  214.7 21.1 %all-to-all-start.7 = ((f32[256,1,128]{2,1,0:T(1,128)}), f32[256,1,128]{2,1,0:T(1,128)S(1)}, u32[]{:S(2)}, u32[]{:S(2)}) async-start(f32[256,1,128]{2,1,0:T(1,128)} %broadcast_in_dim.53), calls=%async_computation.7 | async-start | bytes 262144 | tf_op jit(solution)/shard_map/all_to_all | solution.py:38

commit v2 on v1

--- a/solution.py
+++ b/solution.py
@@ -55,8 +55,7 @@
     grad_total = sum_over_user(partial_grad)
     tile_wide = tile_rows.astype(jnp.float32)
     new_factors = tile_wide - learn_rate * (grad_total + factor_decay * tile_wide)
-    own_tile = jnp.where(user_pos == 0, tile_wide - learn_rate * factor_decay * tile_wide, 0.0)
-    share = learn_rate * partial_grad - own_tile
+    share = jnp.where(user_pos == 0, -new_factors, 0.0)
     items = item_factors.shape[0]
     minus_targets = jnp.zeros((items, share.shape[1]), jnp.float32).at[local_index].set(share)
     total_features = features.shape[1] * devices_all

time: 243 us -> 247 us (1.016)
  blocking collectives: 65.6 us -> 163 us
  waiting for transfers between devices: 94.4 us -> 29.5 us
  starting transfers between devices: 35 us -> 8.9 us
    all_to_all x3 -> x0, waiting for transfers between devices: 50.8 us -> none  [the longest x1 30.6 us: reduce_scatter_rows(): return lax.all_to_all(blocks, ALL, 0, 0, tiled=True).sum(0)]
    all_to_all x0 -> x2, blocking collectives: none -> 48.3 us  [the longest x1 26.2 us: gather_rows(): got = lax.all_to_all(sent, ALL, 0, 0, tiled=True)]
    all_to_all x1 -> x2, blocking collectives: 47.4 us -> 78.7 us  [reduce_scatter_rows(): return lax.all_to_all(blocks, ALL, 0, 0, tiled=True).sum(0)]
    all_to_all x2 -> x1, waiting for transfers between devices: 40.9 us -> 19.7 us  [gather_rows(): got = lax.all_to_all(sent, ALL, 0, 0, tiled=True)]
    all_to_all x3 -> x0, starting transfers between devices: 20 us -> none  [the longest x1 8.29 us: total_scalar(): return lax.all_to_all(sent, ALL, 0, 0, tiled=True).sum(0)[0, 0]]
    all_to_all x1 -> x2, blocking collectives: 18.1 us -> 36.3 us  [total_scalar(): return lax.all_to_all(sent, ALL, 0, 0, tiled=True).sum(0)[0, 0]]
    all_to_all x1, waiting for transfers between devices: 2.69 us -> 9.79 us  [sum_over_user(): return lax.all_to_all(sent, 'user', 0, 0, tiled=True).reshape(x.shape)]
    all_to_all x2 -> x1, starting transfers between devices: 11.2 us -> 5.17 us  [gather_rows(): got = lax.all_to_all(sent, ALL, 0, 0, tiled=True)]
  transfers between devices with their start and end apart: 6 -> 2, of which waited for: 6 -> 2; matrix products, arithmetic and copies ran while one was open for 5% -> 1% of each run, Pallas kernels for 0% -> 0%
where the time goes in v2:
time: 247 us; the launch traced here: 246 us
  blocking collectives  163 us (66%)
  waiting for transfers between devices  29.5 us (12%)
  matrix products  22.4 us (9%)
  local copies, waits for them, and re-layouts  13.8 us (6%)
  starting transfers between devices  8.9 us (4%)
  other arithmetic  7.64 us (3%)
    all_to_all x2, blocking collectives, reduce_scatter_rows(): return lax.all_to_all(blocks, ALL, 0, 0, tiled=True).sum(0)  78.7 us
    all_to_all x2, blocking collectives, total_scalar(): return lax.all_to_all(sent, ALL, 0, 0, tiled=True).sum(0)[0, 0]  36.3 us
    all_to_all x1, blocking collectives, gather_rows(): got = lax.all_to_all(sent, ALL, 0, 0, tiled=True)  26.2 us
    all_to_all x1, blocking collectives, sum_over_user(): block = lax.all_to_all(blocks, 'user', 0, 0, tiled=True).sum(0)  22.1 us
    all_to_all x1, waiting for transfers between devices, gather_rows(): got = lax.all_to_all(sent, ALL, 0, 0, tiled=True)  19.7 us
    dot_general x2, matrix products, local(): lax.dot_general(features, error_rows, (((0,), (0,)), ((), ())), preferred...  10.7 us
    dot_general x2, matrix products, local(): jnp.dot(features, weights_bf, preferred_element_type=jnp.float32)  9.86 us
    all_to_all x1, waiting for transfers between devices, sum_over_user(): return lax.all_to_all(sent, 'user', 0, 0, tiled=True).reshape(x.shape)  9.79 us
  transfers between devices with their start and end apart: 2, of which 2 were waited for; matrix products, arithmetic and copies ran while one was open for 1% of the time, Pallas kernels for 0%

profile of v2, /device:TPU:1, one launch (start us, length us, event | category | flops | bytes accessed | tf_op | source)
XLA Modules:
  0.0 246.4 jit_solution(17641084112151154905)
XLA Ops:
  2.4 1.8 fusion.9
  4.3 22.1 %all_to_all.40 = f32[16,4,256]{2,1,0:T(4,128)S(1)} all-to-all(f32[16,4,256]{2,1,0:T(4,128)S(1)} %reshape.50), channel_id=1, replica_groups=mesh['user'=16,'party'=16] {'user'}, dimensions={0} | all-to-all | bytes 131072 | tf_op jit(solution)/shard_map/all_to_all | solution.py:31
  27.0 3.7 %all-to-all-start.1 = ((f32[16,4,256]{2,1,0:T(4,128)}), f32[16,4,256]{2,1,0:T(4,128)S(1)}, u32[]{:S(2)}, u32[]{:S(2)}) async-start(f32[16,4,256]{2,1,0:T(4,128)} %broadcast_in_dim.47), calls=%async_computation.1 | async-start | bytes 131072 | tf_op jit(solution)/shard_map/all_to_all | solution.py:33
  30.8 9.8 %all-to-all-done.1 = f32[16,4,256]{2,1,0:T(4,128)S(1)} async-done(((f32[16,4,256]{2,1,0:T(4,128)}), f32[16,4,256]{2,1,0:T(4,128)S(1)}, u32[]{:S(2)}, u32[]{:S(2)}) %all-to-all-start.1) | async-done | bytes 65568 | tf_op jit(solution)/shard_map/all_to_all | solution.py:33
  40.7 1.1 scatter_custom_fusion
  41.8 4.8 %fusion.5 = f32[1024,256]{1,0:T(8,128)} fusion(f32[1024,256]{1,0:T(8,128)S(1)} %scatter_custom_fusion, bf16[1024,2048]{1,0:T(8,128)(2,1)} %param.12, bf16[2048,256]{1,0:T(8,128)(2,1)S(1)} %copy-done.2), kind=kOutput, calls=%fused_computation.16 | convolution fusion | flops 1074266112 | bytes 7340032 | tf_op jit(solution)/shard_map/dot_general | solution.py:67
  46.6 1.5 reshape.52
  48.1 39.1 %all_to_all.41 = f32[256,4,256]{2,1,0:T(4,128)S(1)} all-to-all(f32[256,4,256]{2,1,0:T(4,128)S(1)} %reshape.52), channel_id=1, replica_groups=mesh['user'=16,'party'=16] {'user','party'}, dimensions={0} | all-to-all | bytes 2097152 | tf_op jit(solution)/shard_map/all_to_all | solution.py:19
  87.5 0.9 broadcast_in_dim.50
  88.5 5.2 %all-to-all-start.3 = ((bf16[256,4,256]{2,1,0:T(4,128)(2,1)}), bf16[256,4,256]{2,1,0:T(4,128)(2,1)S(1)}, u32[]{:S(2)}, u32[]{:S(2)}) async-start(bf16[256,4,256]{2,1,0:T(4,128)(2,1)} %broadcast_in_dim.50), calls=%async_computation.3 | async-start | bytes 1048576 | tf_op jit(solution)/shard_map/all_to_all | solution.py:24
  93.6 1.4 copy.15
  95.1 19.7 %all-to-all-done.3 = bf16[256,4,256]{2,1,0:T(4,128)(2,1)S(1)} async-done(((bf16[256,4,256]{2,1,0:T(4,128)(2,1)}), bf16[256,4,256]{2,1,0:T(4,128)(2,1)S(1)}, u32[]{:S(2)}, u32[]{:S(2)}) %all-to-all-start.3) | async-done | bytes 524320 | tf_op jit(solution)/shard_map/all_to_all | solution.py:24
  114.9 4.7 %multiply_reduce_fusion.1 = (f32[]{:T(128)}, f32[2048,256]{0,1:T(8,128)S(1)}) fusion(bf16[2048,256]{0,1:T(8,128)(2,1)} %copy.15, bf16[1024,256]{1,0:T(8,128)(2,1)S(1)} %reshape.53, bf16[1024,2048]{1,0:T(8,128)(2,1)} %param.12), kind=kOutput, calls=%fused_computation.12 | convolution fusion | flops 1076887552 | bytes 7864324 | tf_op jit(solution)/shard_map/dot_general | solution.py:72
  120.3 18.1 %all_to_all.42 = f32[256,1,128]{2,1,0:T(1,128)S(1)} all-to-all(f32[256,1,128]{2,1,0:T(1,128)S(1)} %broadcast_in_dim.51), channel_id=1, replica_groups=mesh['user'=16,'party'=16] {'user','party'}, dimensions={0} | all-to-all | bytes 262144 | tf_op jit(solution)/shard_map/all_to_all | solution.py:38
  138.6 5.1 %fusion.6 = f32[1024,256]{1,0:T(8,128)} fusion(f32[1024,256]{1,0:T(8,128)} %copy-done.1, bf16[1024,2048]{1,0:T(8,128)(2,1)} %param.12, bf16[2048,256]{0,1:T(8,128)(2,1)} %copy.15, f32[2048,256]{0,1:T(8,128)S(1)} %get-tuple-element.11, f32[]{:T(128)} %bitcast.3), kind=kOutput, calls=%fused_computation.17 | convolution fusion | flops 1076363264 | bytes 9437188 | tf_op jit(solution)/shard_map/dot_general | solution.py:67
  143.6 2.5 %reshape.54 = f32[256,4,256]{2,1,0:T(4,128)} reshape(f32[1024,256]{1,0:T(8,128)} %fusion.6) | data formatting | bytes 2097152 | tf_op jit(solution)/shard_map/reshape | solution.py:18
  146.1 39.6 %all_to_all.43 = f32[256,4,256]{2,1,0:T(4,128)} all-to-all(f32[256,4,256]{2,1,0:T(4,128)} %reshape.54), channel_id=1, replica_groups=mesh['user'=16,'party'=16] {'user','party'}, dimensions={0} | all-to-all | bytes 2097152 | tf_op jit(solution)/shard_map/all_to_all | solution.py:19
  185.7 1.5 reduce_sum.72
  187.4 26.2 %all_to_all.44 = bf16[256,4,256]{2,1,0:T(4,128)(2,1)} all-to-all(bf16[256,4,256]{2,1,0:T(4,128)(2,1)S(1)} %broadcast_in_dim.52), channel_id=1, replica_groups=mesh['user'=16,'party'=16] {'user','party'}, dimensions={0} | all-to-all | bytes 1048576 | tf_op jit(solution)/shard_map/all_to_all | solution.py:24
  213.6 1.2 reshape.55
  214.8 6.0 %multiply_reduce_fusion = (f32[]{:T(128)}, f32[2048,256]{0,1:T(8,128)}) fusion(f32[2048,256]{0,1:T(8,128)S(1)} %get-tuple-element.11, f32[]{:T(128)} %bitcast.3, bf16[2048,256]{0,1:T(8,128)(2,1)} %copy.15, bf16[1024,256]{1,0:T(8,128)(2,1)S(1)} %reshape.55, bf16[1024,2048]{1,0:T(8,128)(2,1)} %param.12), kind=kOutput, calls=%fused_computation.11 | convolution fusion | flops 1077936128 | bytes 9961480 | tf_op jit(solution)/shard_map/dot_general | solution.py:72
  221.5 18.1 %all_to_all.45 = f32[256,1,128]{2,1,0:T(1,128)S(1)} all-to-all(f32[256,1,128]{2,1,0:T(1,128)S(1)} %broadcast_in_dim.53), channel_id=1, replica_groups=mesh['user'=16,'party'=16] {'user','party'}, dimensions={0} | all-to-all | bytes 262144 | tf_op jit(solution)/shard_map/all_to_all | solution.py:38
  239.8 3.7 %multiply_subtract_fusion = f32[2048,256]{0,1:T(8,128)} fusion(f32[2048,256]{0,1:T(8,128)} %get-tuple-element.13, f32[]{:T(128)} %bitcast.8, f32[2048,256]{0,1:T(8,128)S(1)} %get-tuple-element.11, f32[]{:T(128)} %bitcast.3, bf16[2048,256]{0,1:T(8,128)(2,1)} %copy.15), kind=kLoop, calls=%fused_computation.10 | loop fusion | flops 2621440 | bytes 7340040 | tf_op jit(solution)/shard_map/sub | solution.py:80
  243.5 2.9 %copy.19 = f32[2048,256]{1,0:T(8,128)} copy(f32[2048,256]{0,1:T(8,128)} %multiply_subtract_fusion) | data formatting | bytes 4194304
  (25 shorter events, 4.7 us)
Async XLA Ops:
  0.6 1.1 copy-start
  0.6 41.1 %copy-start.2 = (bf16[2048,256]{1,0:T(8,128)(2,1)S(1)}, bf16[2048,256]{1,0:T(8,128)(2,1)}, u32[]{:S(2)}) copy-start(bf16[2048,256]{1,0:T(8,128)(2,1)} %param.13) | copy-start | bytes 3145732
  27.0 13.5 %all-to-all-start.1 = ((f32[16,4,256]{2,1,0:T(4,128)}), f32[16,4,256]{2,1,0:T(4,128)S(1)}, u32[]{:S(2)}, u32[]{:S(2)}) async-start(f32[16,4,256]{2,1,0:T(4,128)} %broadcast_in_dim.47), calls=%async_computation.1 | async-start | bytes 131072 | tf_op jit(solution)/shard_map/all_to_all | solution.py:33
  40.7 5.9 %copy-start.4 = (f32[64,256]{1,0:T(8,128)}, f32[64,256]{1,0:T(8,128)S(1)}, u32[]{:S(2)}) copy-start(f32[64,256]{1,0:T(8,128)S(1)} %convert_subtract_fusion.2) | copy-start | bytes 196612
  41.8 4.8 %copy-start.1 = (f32[1024,256]{1,0:T(8,128)}, f32[1024,256]{1,0:T(8,128)S(1)}, u32[]{:S(2)}) copy-start(f32[1024,256]{1,0:T(8,128)S(1)} %scatter_custom_fusion) | copy-start | bytes 3145732
  87.2 6.4 %copy-start.3 = (bf16[2048,256]{1,0:T(8,128)(2,1)S(1)}, bf16[2048,256]{1,0:T(8,128)(2,1)}, u32[]{:S(2)}) copy-start(bf16[2048,256]{1,0:T(8,128)(2,1)} %param.13) | copy-start | bytes 3145732
  88.5 26.3 %all-to-all-start.3 = ((bf16[256,4,256]{2,1,0:T(4,128)(2,1)}), bf16[256,4,256]{2,1,0:T(4,128)(2,1)S(1)}, u32[]{:S(2)}, u32[]{:S(2)}) async-start(bf16[256,4,256]{2,1,0:T(4,128)(2,1)} %broadcast_in_dim.50), calls=%async_computation.3 | async-start | bytes 1048576 | tf_op jit(solution)/shard_map/all_to_all | solution.py:24

commit v3 on v1

--- a/solution.py
+++ b/solution.py
@@ -25,20 +25,12 @@
     return got.reshape(n * block.shape[0], block.shape[1])
 
 
-def sum_over_user(x):
-    n = lax.axis_size("user")
-    blocks = x.reshape(n, x.shape[0] // n, x.shape[1])
-    block = lax.all_to_all(blocks, "user", 0, 0, tiled=True).sum(0)
-    sent = jnp.broadcast_to(block[None], (n,) + block.shape)
-    return lax.all_to_all(sent, "user", 0, 0, tiled=True).reshape(x.shape)
-
-
 def total_scalar(value, n):
     sent = jnp.broadcast_to(value, (n, 1, 128))
     return lax.all_to_all(sent, ALL, 0, 0, tiled=True).sum(0)[0, 0]
 
 
-def local(ratings, rating_mask, user_factors, item_factors, item_index, features, ridge_weights):
+def body(ratings, rating_mask, user_factors, item_factors, item_index, features, ridge_weights):
     local_items = ratings.shape[0]
     party_pos = lax.axis_index("party")
     user_pos = lax.axis_index("user")
@@ -52,7 +44,7 @@
         jnp.bfloat16
     )
     partial_grad = jnp.dot(misfit, user_factors, preferred_element_type=jnp.float32)
-    grad_total = sum_over_user(partial_grad)
+    grad_total = lax.psum(partial_grad, "user")
     tile_wide = tile_rows.astype(jnp.float32)
     new_factors = tile_wide - learn_rate * (grad_total + factor_decay * tile_wide)
     own_tile = jnp.where(user_pos == 0, tile_wide - learn_rate * factor_decay * tile_wide, 0.0)
@@ -62,7 +54,7 @@
     total_features = features.shape[1] * devices_all
     feature_scale = 1.0 / float(total_features) ** 0.5
     weights = ridge_weights.astype(jnp.float32)
-    for iteration in range(ITERS):
+    for _ in range(ITERS):
         weights_bf = weights.astype(jnp.bfloat16)
         partial_pred = (
             jnp.dot(features, weights_bf, preferred_element_type=jnp.float32) * feature_scale
@@ -93,4 +85,4 @@
         P(ALL, None),
     )
     out_specs = (P("party", None), P(ALL, None))
-    return jax.shard_map(local, mesh=mesh, in_specs=in_specs, out_specs=out_specs, check_vma=False)
+    return jax.shard_map(body, mesh=mesh, in_specs=in_specs, out_specs=out_specs, check_vma=False)

time: 243 us -> 361 us (1.49)
  waiting for transfers between devices: 94.4 us -> 177 us
  blocking collectives: 65.6 us -> 105 us
  starting transfers between devices: 35 us -> 17.6 us
  between operations: 0.95 us -> 14.3 us
    psum x0 -> x1, waiting for transfers between devices: none -> 138 us  [body(): grad_total = lax.psum(partial_grad, 'user')]
    all_to_all x3 -> x0, waiting for transfers between devices: 41.5 us -> none  [the longest x1 30.6 us: reduce_scatter_rows(): return lax.all_to_all(blocks, ALL, 0, 0, tiled=True).sum(0)]
    all_to_all x1 -> x2, blocking collectives: 47.4 us -> 86.8 us  [reduce_scatter_rows(): return lax.all_to_all(blocks, ALL, 0, 0, tiled=True).sum(0)]
    all_to_all x3 -> x0, starting transfers between devices: 15.5 us -> none  [the longest x1 7.63 us: reduce_scatter_rows(): return lax.all_to_all(blocks, ALL, 0, 0, tiled=True).sum(0)]
    all_to_all x1, waiting for transfers between devices: 12 us -> 0.01 us  [total_scalar(): return lax.all_to_all(sent, ALL, 0, 0, tiled=True).sum(0)[0, 0]]
  transfers between devices with their start and end apart: 6 -> 4, of which waited for: 6 -> 3; matrix products, arithmetic and copies ran while one was open for 5% -> 3% of each run, Pallas kernels for 0% -> 0%
where the time goes in v3:
time: 361 us; the launch traced here: 360 us
  waiting for transfers between devices  177 us (49%)
  blocking collectives  105 us (29%)
  matrix products  22.3 us (6%)
  starting transfers between devices  17.6 us (5%)
  local copies, waits for them, and re-layouts  14.4 us (4%)
  between operations  14.3 us (4%)
  other arithmetic  9.31 us (3%)
    psum x1, waiting for transfers between devices, body(): grad_total = lax.psum(partial_grad, 'user')  138 us
    all_to_all x2, blocking collectives, reduce_scatter_rows(): return lax.all_to_all(blocks, ALL, 0, 0, tiled=True).sum(0)  86.8 us
    all_to_all x2, waiting for transfers between devices, gather_rows(): got = lax.all_to_all(sent, ALL, 0, 0, tiled=True)  38.6 us
    all_to_all x1, blocking collectives, total_scalar(): return lax.all_to_all(sent, ALL, 0, 0, tiled=True).sum(0)[0, 0]  18.1 us
    all_to_all x2, starting transfers between devices, gather_rows(): got = lax.all_to_all(sent, ALL, 0, 0, tiled=True)  12 us
    dot_general x2, matrix products, body(): lax.dot_general(features, error_rows, (((0,), (0,)), ((), ())), preferred...  10.6 us
    dot_general x2, matrix products, body(): jnp.dot(features, weights_bf, preferred_element_type=jnp.float32)  9.86 us
  transfers between devices with their start and end apart: 4, of which 3 were waited for; matrix products, arithmetic and copies ran while one was open for 3% of the time, Pallas kernels for 0%

profile of v3, /device:TPU:1, one launch (start us, length us, event | category | flops | bytes accessed | tf_op | source)
XLA Modules:
  0.0 359.7 jit_solution(9040377369440600085)
XLA Ops:
  8.9 1.8 fusion.9
  10.8 1.1 scatter_custom_fusion
  11.9 4.8 %fusion.5 = f32[1024,256]{1,0:T(8,128)} fusion(f32[1024,256]{1,0:T(8,128)S(1)} %scatter_custom_fusion, bf16[1024,2048]{1,0:T(8,128)(2,1)} %param.12, bf16[2048,256]{1,0:T(8,128)(2,1)S(1)} %copy-done.2), kind=kOutput, calls=%fused_computation.16 | convolution fusion | flops 1074266112 | bytes 7340032 | tf_op jit(solution)/shard_map/dot_general | solution.py:60
  16.7 1.5 reshape.43
  18.3 47.4 %all_to_all.30 = f32[256,4,256]{2,1,0:T(4,128)S(1)} all-to-all(f32[256,4,256]{2,1,0:T(4,128)S(1)} %reshape.43), channel_id=1, replica_groups=mesh['user'=16,'party'=16] {'user','party'}, dimensions={0} | all-to-all | bytes 2097152 | tf_op jit(solution)/shard_map/all_to_all | solution.py:19
  66.9 5.2 %all-to-all-start.1 = ((bf16[256,4,256]{2,1,0:T(4,128)(2,1)}), bf16[256,4,256]{2,1,0:T(4,128)(2,1)S(1)}, u32[]{:S(2)}, u32[]{:S(2)}) async-start(bf16[256,4,256]{2,1,0:T(4,128)(2,1)} %broadcast_in_dim.43), calls=%async_computation.1 | async-start | bytes 1048576 | tf_op jit(solution)/shard_map/all_to_all | solution.py:24
  72.1 1.4 copy.15
  73.6 19.7 %all-to-all-done.1 = bf16[256,4,256]{2,1,0:T(4,128)(2,1)S(1)} async-done(((bf16[256,4,256]{2,1,0:T(4,128)(2,1)}), bf16[256,4,256]{2,1,0:T(4,128)(2,1)S(1)}, u32[]{:S(2)}, u32[]{:S(2)}) %all-to-all-start.1) | async-done | bytes 524320 | tf_op jit(solution)/shard_map/all_to_all | solution.py:24
  93.4 4.7 %multiply_reduce_fusion.1 = (f32[]{:T(128)}, f32[2048,256]{0,1:T(8,128)S(1)}) fusion(bf16[2048,256]{0,1:T(8,128)(2,1)} %copy.15, bf16[1024,256]{1,0:T(8,128)(2,1)S(1)} %reshape.44, bf16[1024,2048]{1,0:T(8,128)(2,1)} %param.12), kind=kOutput, calls=%fused_computation.12 | convolution fusion | flops 1076887552 | bytes 7864324 | tf_op jit(solution)/shard_map/dot_general | solution.py:65
  98.8 18.1 %all_to_all.31 = f32[256,1,128]{2,1,0:T(1,128)S(1)} all-to-all(f32[256,1,128]{2,1,0:T(1,128)S(1)} %broadcast_in_dim.44), channel_id=1, replica_groups=mesh['user'=16,'party'=16] {'user','party'}, dimensions={0} | all-to-all | bytes 262144 | tf_op jit(solution)/shard_map/all_to_all | solution.py:30
  117.0 5.1 %fusion.6 = f32[1024,256]{1,0:T(8,128)} fusion(f32[1024,256]{1,0:T(8,128)} %copy-done.1, bf16[1024,2048]{1,0:T(8,128)(2,1)} %param.12, bf16[2048,256]{0,1:T(8,128)(2,1)} %copy.15, f32[2048,256]{0,1:T(8,128)S(1)} %get-tuple-element.11, f32[]{:T(128)} %bitcast.3), kind=kOutput, calls=%fused_computation.17 | convolution fusion | flops 1076363264 | bytes 9437188 | tf_op jit(solution)/shard_map/dot_general | solution.py:60
  122.1 2.5 reshape.45
  124.6 39.4 %all_to_all.32 = f32[256,4,256]{2,1,0:T(4,128)} all-to-all(f32[256,4,256]{2,1,0:T(4,128)} %reshape.45), channel_id=1, replica_groups=mesh['user'=16,'party'=16] {'user','party'}, dimensions={0} | all-to-all | bytes 2097152 | tf_op jit(solution)/shard_map/all_to_all | solution.py:19
  164.0 1.5 reduce_sum.62
  166.5 6.8 %all-to-all-start.4 = ((bf16[256,4,256]{2,1,0:T(4,128)(2,1)}), bf16[256,4,256]{2,1,0:T(4,128)(2,1)}, u32[]{:S(2)}, u32[]{:S(2)}) async-start(bf16[256,4,256]{2,1,0:T(4,128)(2,1)} %broadcast_in_dim.45), calls=%async_computation.4 | async-start | bytes 1048576 | tf_op jit(solution)/shard_map/all_to_all | solution.py:24
  174.0 19.0 %all-to-all-done.4 = bf16[256,4,256]{2,1,0:T(4,128)(2,1)} async-done(((bf16[256,4,256]{2,1,0:T(4,128)(2,1)}), bf16[256,4,256]{2,1,0:T(4,128)(2,1)}, u32[]{:S(2)}, u32[]{:S(2)}) %all-to-all-start.4) | async-done | bytes 524320 | tf_op jit(solution)/shard_map/all_to_all | solution.py:24
  193.0 1.2 reshape.46
  194.1 5.9 %multiply_reduce_fusion = (f32[]{:T(128)}, f32[2048,256]{0,1:T(8,128)}) fusion(f32[2048,256]{0,1:T(8,128)S(1)} %get-tuple-element.11, f32[]{:T(128)} %bitcast.3, bf16[2048,256]{0,1:T(8,128)(2,1)} %copy.15, bf16[1024,256]{1,0:T(8,128)(2,1)S(1)} %reshape.46, bf16[1024,2048]{1,0:T(8,128)(2,1)} %param.12), kind=kOutput, calls=%fused_computation.11 | convolution fusion | flops 1077936128 | bytes 9961480 | tf_op jit(solution)/shard_map/dot_general | solution.py:65
  200.1 1.3 broadcast_in_dim.46
  201.3 5.6 %all-to-all-start.5 = ((f32[256,1,128]{2,1,0:T(1,128)}), f32[256,1,128]{2,1,0:T(1,128)S(1)}, u32[]{:S(2)}, u32[]{:S(2)}) async-start(f32[256,1,128]{2,1,0:T(1,128)} %broadcast_in_dim.46), calls=%async_computation.5 | async-start | bytes 262144 | tf_op jit(solution)/shard_map/all_to_all | solution.py:30
  206.9 137.5 %all-reduce.2.cloned.1.call-done = f32[64,256]{1,0:T(8,128)} async-done(((f32[64,256]{1,0:T(8,128)}), f32[64,256]{1,0:T(8,128)}) %all-reduce.2.cloned.1.call-update) | async-done | bytes 65552 | tf_op jit(solution)/shard_map/psum | solution.py:47
  344.4 1.5 convert_subtract_fusion.3
  346.1 3.8 %multiply_subtract_fusion = f32[2048,256]{0,1:T(8,128)} fusion(f32[2048,256]{0,1:T(8,128)} %get-tuple-element.13, f32[]{:T(128)} %bitcast.8, f32[2048,256]{0,1:T(8,128)S(1)} %get-tuple-element.11, f32[]{:T(128)} %bitcast.3, bf16[2048,256]{0,1:T(8,128)(2,1)} %copy.15), kind=kLoop, calls=%fused_computation.10 | loop fusion | flops 2621440 | bytes 7340040 | tf_op jit(solution)/shard_map/sub | solution.py:73
  349.9 2.9 copy.19
  (23 shorter events, 5.6 us)
Async XLA Ops:
  7.2 1.1 copy-start
  7.2 4.7 %copy-start.2 = (bf16[2048,256]{1,0:T(8,128)(2,1)S(1)}, bf16[2048,256]{1,0:T(8,128)(2,1)}, u32[]{:S(2)}) copy-start(bf16[2048,256]{1,0:T(8,128)(2,1)} %param.13) | copy-start | bytes 3145732
  10.8 6.0 %copy-start.4 = (f32[64,256]{1,0:T(8,128)}, f32[64,256]{1,0:T(8,128)S(1)}, u32[]{:S(2)}) copy-start(f32[64,256]{1,0:T(8,128)S(1)} %fusion.9) | copy-start | bytes 196612
  11.9 4.8 %copy-start.1 = (f32[1024,256]{1,0:T(8,128)}, f32[1024,256]{1,0:T(8,128)S(1)}, u32[]{:S(2)}) copy-start(f32[1024,256]{1,0:T(8,128)S(1)} %scatter_custom_fusion) | copy-start | bytes 3145732
  65.7 6.4 %copy-start.3 = (bf16[2048,256]{1,0:T(8,128)(2,1)S(1)}, bf16[2048,256]{1,0:T(8,128)(2,1)}, u32[]{:S(2)}) copy-start(bf16[2048,256]{1,0:T(8,128)(2,1)} %param.13) | copy-start | bytes 3145732
  66.9 26.3 %all-to-all-start.1 = ((bf16[256,4,256]{2,1,0:T(4,128)(2,1)}), bf16[256,4,256]{2,1,0:T(4,128)(2,1)S(1)}, u32[]{:S(2)}, u32[]{:S(2)}) async-start(bf16[256,4,256]{2,1,0:T(4,128)(2,1)} %broadcast_in_dim.43), calls=%async_computation.1 | async-start | bytes 1048576 | tf_op jit(solution)/shard_map/all_to_all | solution.py:24
  166.5 26.5 %all-to-all-start.4 = ((bf16[256,4,256]{2,1,0:T(4,128)(2,1)}), bf16[256,4,256]{2,1,0:T(4,128)(2,1)}, u32[]{:S(2)}, u32[]{:S(2)}) async-start(bf16[256,4,256]{2,1,0:T(4,128)(2,1)} %broadcast_in_dim.45), calls=%async_computation.4 | async-start | bytes 1048576 | tf_op jit(solution)/shard_map/all_to_all | solution.py:24
  173.3 171.1 %all-reduce.2.cloned.1.call-start = ((), (), s32[]{:S(2)}) async-start(), calls=%async_computation.6 | async-start | bytes 131072 | tf_op jit(solution)/shard_map/psum | solution.py:47
  201.3 144.6 %all-to-all-start.5 = ((f32[256,1,128]{2,1,0:T(1,128)}), f32[256,1,128]{2,1,0:T(1,128)S(1)}, u32[]{:S(2)}, u32[]{:S(2)}) async-start(f32[256,1,128]{2,1,0:T(1,128)} %broadcast_in_dim.46), calls=%async_computation.5 | async-start | bytes 262144 | tf_op jit(solution)/shard_map/all_to_all | solution.py:30
Sparse Core Ops, SparseCore 0:
  177.3 167.0 all-reduce.1

commit v4 on v3

--- a/solution.py
+++ b/solution.py
@@ -14,15 +14,17 @@
 ALL = ("user", "party")
 
 
-def reduce_scatter_rows(x, n):
-    blocks = x.reshape(n, x.shape[0] // n, x.shape[1])
-    return lax.all_to_all(blocks, ALL, 0, 0, tiled=True).sum(0)
+def reduce_scatter_tiles(x, n):
+    rows, cols = x.shape
+    tiles = x.reshape(rows // 8, 8, cols // 128, 128).transpose(0, 2, 1, 3).reshape(n, 8, 128)
+    return lax.all_to_all(tiles, ALL, 0, 0, tiled=True).sum(0)
 
 
-def gather_rows(block, n):
+def gather_tiles(block, n, shape):
+    rows, cols = shape
     sent = jnp.broadcast_to(block[None], (n,) + block.shape)
     got = lax.all_to_all(sent, ALL, 0, 0, tiled=True)
-    return got.reshape(n * block.shape[0], block.shape[1])
+    return got.reshape(rows // 8, cols // 128, 8, 128).transpose(0, 2, 1, 3).reshape(rows, cols)
 
 
 def total_scalar(value, n):
@@ -59,8 +61,8 @@
         partial_pred = (
             jnp.dot(features, weights_bf, preferred_element_type=jnp.float32) * feature_scale
         )
-        error_block = reduce_scatter_rows(partial_pred + minus_targets, devices_all)
-        error_rows = gather_rows(error_block.astype(jnp.bfloat16), devices_all)
+        error_block = reduce_scatter_tiles(partial_pred + minus_targets, devices_all)
+        error_rows = gather_tiles(error_block.astype(jnp.bfloat16), devices_all, partial_pred.shape)
         grad = (
             lax.dot_general(
                 features, error_rows, (((0,), (0,)), ((), ())), preferred_element_type=jnp.float32

time: 361 us -> 352 us (0.975)
  local copies, waits for them, and re-layouts: 14.4 us -> 8.99 us
    reshape x4 -> x0, local copies, waits for them, and re-layouts: 5.34 us -> none  [the longest x2 4.05 us: reduce_scatter_rows(): blocks = x.reshape(n, x.shape[0] // n, x.shape[1])]
where the time goes in v4:
time: 352 us
  waiting for transfers between devices  178 us (51%)
  blocking collectives  104 us (30%)
  matrix products  20.5 us (6%)
  starting transfers between devices  16.1 us (5%)
  between operations  14.3 us (4%)
  other arithmetic  9.29 us (3%)
  local copies, waits for them, and re-layouts  8.99 us (3%)
    psum x1, waiting for transfers between devices, body(): grad_total = lax.psum(partial_grad, 'user')  138 us
    all_to_all x2, blocking collectives, reduce_scatter_tiles(): return lax.all_to_all(tiles, ALL, 0, 0, tiled=True).sum(0)  86 us
    all_to_all x2, waiting for transfers between devices, gather_tiles(): got = lax.all_to_all(sent, ALL, 0, 0, tiled=True)  39.9 us
    all_to_all x1, blocking collectives, total_scalar(): return lax.all_to_all(sent, ALL, 0, 0, tiled=True).sum(0)[0, 0]  18.1 us
    dot_general x2, matrix products, body(): lax.dot_general(features, error_rows, (((0,), (0,)), ((), ())), preferred...  10.7 us
    all_to_all x2, starting transfers between devices, gather_tiles(): got = lax.all_to_all(sent, ALL, 0, 0, tiled=True)  10.5 us
    dot_general x2, matrix products, body(): jnp.dot(features, weights_bf, preferred_element_type=jnp.float32)  7.91 us
  transfers between devices with their start and end apart: 4, of which 3 were waited for; matrix products, arithmetic and copies ran while one was open for 3% of the time, Pallas kernels for 0%

profile of v4, /device:TPU:1, one launch (start us, length us, event | category | flops | bytes accessed | tf_op | source)
XLA Modules:
  0.0 351.6 jit_solution(16730195439434647932)
XLA Ops:
  7.2 0.9 compare_and_fusion
  8.9 1.8 fusion.9
  10.8 1.1 scatter_custom_fusion
  11.9 3.8 %fusion.5 = f32[1024,256]{1,0:T(8,128)S(1)} fusion(f32[1024,256]{1,0:T(8,128)S(1)} %scatter_custom_fusion, bf16[1024,2048]{1,0:T(8,128)(2,1)} %param.12, bf16[2048,256]{1,0:T(8,128)(2,1)S(1)} %copy-done.2), kind=kOutput, calls=%fused_computation.16 | convolution fusion | flops 1074266112 | bytes 7340032 | tf_op jit(solution)/shard_map/dot_general | solution.py:62
  15.8 47.4 %all_to_all.30 = f32[256,8,128]{2,1,0:T(8,128)S(1)} all-to-all(f32[256,8,128]{2,1,0:T(8,128)S(1)} %bitcast.53), channel_id=1, replica_groups=mesh['user'=16,'party'=16] {'user','party'}, dimensions={0} | all-to-all | bytes 2097152 | tf_op jit(solution)/shard_map/all_to_all | solution.py:20
  63.5 0.9 broadcast_in_dim.43
  64.4 5.1 %all-to-all-start.1 = ((bf16[256,8,128]{2,1,0:T(8,128)(2,1)}), bf16[256,8,128]{2,1,0:T(8,128)(2,1)S(1)}, u32[]{:S(2)}, u32[]{:S(2)}) async-start(bf16[256,8,128]{2,1,0:T(8,128)(2,1)} %broadcast_in_dim.43), calls=%async_computation.1 | async-start | bytes 1048576 | tf_op jit(solution)/shard_map/all_to_all | solution.py:26
  69.5 1.4 copy.15
  71.0 19.7 %all-to-all-done.1 = bf16[256,8,128]{2,1,0:T(8,128)(2,1)S(1)} async-done(((bf16[256,8,128]{2,1,0:T(8,128)(2,1)}), bf16[256,8,128]{2,1,0:T(8,128)(2,1)S(1)}, u32[]{:S(2)}, u32[]{:S(2)}) %all-to-all-start.1) | async-done | bytes 524320 | tf_op jit(solution)/shard_map/all_to_all | solution.py:26
  90.7 4.7 %multiply_reduce_fusion.1 = (f32[]{:T(128)}, f32[2048,256]{0,1:T(8,128)S(1)}) fusion(bf16[2048,256]{0,1:T(8,128)(2,1)} %copy.15, bf16[1024,256]{1,0:T(8,128)(2,1)S(1)} %bitcast.51, bf16[1024,2048]{1,0:T(8,128)(2,1)} %param.12), kind=kOutput, calls=%fused_computation.12 | convolution fusion | flops 1076887552 | bytes 7864324 | tf_op jit(solution)/shard_map/dot_general | solution.py:67
  96.2 18.1 %all_to_all.31 = f32[256,1,128]{2,1,0:T(1,128)S(1)} all-to-all(f32[256,1,128]{2,1,0:T(1,128)S(1)} %broadcast_in_dim.44), channel_id=1, replica_groups=mesh['user'=16,'party'=16] {'user','party'}, dimensions={0} | all-to-all | bytes 262144 | tf_op jit(solution)/shard_map/all_to_all | solution.py:32
  114.5 4.1 %fusion.6 = f32[1024,256]{1,0:T(8,128)S(1)} fusion(f32[1024,256]{1,0:T(8,128)} %copy-done.1, bf16[1024,2048]{1,0:T(8,128)(2,1)} %param.12, bf16[2048,256]{0,1:T(8,128)(2,1)} %copy.15, f32[2048,256]{0,1:T(8,128)S(1)} %get-tuple-element.11, f32[]{:T(128)} %bitcast.9), kind=kOutput, calls=%fused_computation.17 | convolution fusion | flops 1076363264 | bytes 9437188 | tf_op jit(solution)/shard_map/dot_general | solution.py:62
  118.5 38.5 %all_to_all.32 = f32[256,8,128]{2,1,0:T(8,128)} all-to-all(f32[256,8,128]{2,1,0:T(8,128)S(1)} %bitcast.50), channel_id=1, replica_groups=mesh['user'=16,'party'=16] {'user','party'}, dimensions={0} | all-to-all | bytes 2097152 | tf_op jit(solution)/shard_map/all_to_all | solution.py:20
  157.1 1.5 reduce_sum.62
  158.6 0.9 broadcast_in_dim.45
  159.4 5.4 %all-to-all-start.4 = ((bf16[256,8,128]{2,1,0:T(8,128)(2,1)}), bf16[256,8,128]{2,1,0:T(8,128)(2,1)S(1)}, u32[]{:S(2)}, u32[]{:S(2)}) async-start(bf16[256,8,128]{2,1,0:T(8,128)(2,1)} %broadcast_in_dim.45), calls=%async_computation.4 | async-start | bytes 1048576 | tf_op jit(solution)/shard_map/all_to_all | solution.py:26
  165.5 20.2 %all-to-all-done.4 = bf16[256,8,128]{2,1,0:T(8,128)(2,1)S(1)} async-done(((bf16[256,8,128]{2,1,0:T(8,128)(2,1)}), bf16[256,8,128]{2,1,0:T(8,128)(2,1)S(1)}, u32[]{:S(2)}, u32[]{:S(2)}) %all-to-all-start.4) | async-done | bytes 524320 | tf_op jit(solution)/shard_map/all_to_all | solution.py:26
  185.8 6.0 %multiply_reduce_fusion = (f32[]{:T(128)}, f32[2048,256]{0,1:T(8,128)}) fusion(f32[2048,256]{0,1:T(8,128)S(1)} %get-tuple-element.11, f32[]{:T(128)} %bitcast.9, bf16[2048,256]{0,1:T(8,128)(2,1)} %copy.15, bf16[1024,256]{1,0:T(8,128)(2,1)S(1)} %bitcast.52, bf16[1024,2048]{1,0:T(8,128)(2,1)} %param.12), kind=kOutput, calls=%fused_computation.11 | convolution fusion | flops 1077936128 | bytes 9961480 | tf_op jit(solution)/shard_map/dot_general | solution.py:67
  191.8 1.3 broadcast_in_dim.46
  193.1 5.6 %all-to-all-start.5 = ((f32[256,1,128]{2,1,0:T(1,128)}), f32[256,1,128]{2,1,0:T(1,128)S(1)}, u32[]{:S(2)}, u32[]{:S(2)}) async-start(f32[256,1,128]{2,1,0:T(1,128)} %broadcast_in_dim.46), calls=%async_computation.5 | async-start | bytes 262144 | tf_op jit(solution)/shard_map/all_to_all | solution.py:32
  198.6 137.7 %all-reduce.2.cloned.1.call-done = f32[64,256]{1,0:T(8,128)} async-done(((f32[64,256]{1,0:T(8,128)}), f32[64,256]{1,0:T(8,128)}) %all-reduce.2.cloned.1.call-update) | async-done | bytes 65552 | tf_op jit(solution)/shard_map/psum | solution.py:49
  336.3 1.5 convert_subtract_fusion.3
  338.0 3.8 %multiply_subtract_fusion = f32[2048,256]{0,1:T(8,128)} fusion(f32[2048,256]{0,1:T(8,128)} %get-tuple-element.13, f32[]{:T(128)} %bitcast.20, f32[2048,256]{0,1:T(8,128)S(1)} %get-tuple-element.11, f32[]{:T(128)} %bitcast.9, bf16[2048,256]{0,1:T(8,128)(2,1)} %copy.15), kind=kLoop, calls=%fused_computation.10 | loop fusion | flops 2621440 | bytes 7340040 | tf_op jit(solution)/shard_map/sub | solution.py:75
  341.8 2.9 copy.19
  (17 shorter events, 2.7 us)
Async XLA Ops:
  7.2 1.1 copy-start
  7.2 4.7 %copy-start.2 = (bf16[2048,256]{1,0:T(8,128)(2,1)S(1)}, bf16[2048,256]{1,0:T(8,128)(2,1)}, u32[]{:S(2)}) copy-start(bf16[2048,256]{1,0:T(8,128)(2,1)} %param.13) | copy-start | bytes 3145732
  10.8 5.0 %copy-start.3 = (f32[64,256]{1,0:T(8,128)}, f32[64,256]{1,0:T(8,128)S(1)}, u32[]{:S(2)}) copy-start(f32[64,256]{1,0:T(8,128)S(1)} %fusion.9) | copy-start | bytes 196612
  11.9 3.9 %copy-start.1 = (f32[1024,256]{1,0:T(8,128)}, f32[1024,256]{1,0:T(8,128)S(1)}, u32[]{:S(2)}) copy-start(f32[1024,256]{1,0:T(8,128)S(1)} %scatter_custom_fusion) | copy-start | bytes 3145732
  64.4 26.3 %all-to-all-start.1 = ((bf16[256,8,128]{2,1,0:T(8,128)(2,1)}), bf16[256,8,128]{2,1,0:T(8,128)(2,1)S(1)}, u32[]{:S(2)}, u32[]{:S(2)}) async-start(bf16[256,8,128]{2,1,0:T(8,128)(2,1)} %broadcast_in_dim.43), calls=%async_computation.1 | async-start | bytes 1048576 | tf_op jit(solution)/shard_map/all_to_all | solution.py:26
  159.4 26.3 %all-to-all-start.4 = ((bf16[256,8,128]{2,1,0:T(8,128)(2,1)}), bf16[256,8,128]{2,1,0:T(8,128)(2,1)S(1)}, u32[]{:S(2)}, u32[]{:S(2)}) async-start(bf16[256,8,128]{2,1,0:T(8,128)(2,1)} %broadcast_in_dim.45), calls=%async_computation.4 | async-start | bytes 1048576 | tf_op jit(solution)/shard_map/all_to_all | solution.py:26
  164.8 171.5 %all-reduce.2.cloned.1.call-start = ((), (), s32[]{:S(2)}) async-start(), calls=%async_computation.6 | async-start | bytes 131072 | tf_op jit(solution)/shard_map/psum | solution.py:49
  193.1 144.8 %all-to-all-start.5 = ((f32[256,1,128]{2,1,0:T(1,128)}), f32[256,1,128]{2,1,0:T(1,128)S(1)}, u32[]{:S(2)}, u32[]{:S(2)}) async-start(f32[256,1,128]{2,1,0:T(1,128)} %broadcast_in_dim.46), calls=%async_computation.5 | async-start | bytes 262144 | tf_op jit(solution)/shard_map/all_to_all | solution.py:32
Sparse Core Ops, SparseCore 0:
  168.8 167.4 all-reduce.1
